TPU v7x, 128 devices: a whole 4x4x4 slice. The times are simulated.
128 devices in a mesh: grp: 4 (over x), tok: 32 (over z, y, core).
Axes of the slice: x: 4, y: 4, z: 4, core: 2. Of those that a mesh axis runs over, the one named last changes fastest.
Arguments:
- tokens: bfloat16 [16384, 2560], P(('grp', 'tok')), may hold values from -6 to 6
- input_gain: bfloat16 [2560], replicated, may hold values from 0.25 to 1.75
- query_down: bfloat16 [2560, 768], replicated, may hold values from -0.125 to 0.125
- query_gain: bfloat16 [768], replicated, may hold values from 0.25 to 1.75
- query_up: bfloat16 [768, 1920], replicated, may hold values from -0.21875 to 0.21875
- latent_down: bfloat16 [2560, 288], replicated, may hold values from -0.125 to 0.125
- latent_gain: bfloat16 [256], replicated, may hold values from 0.25 to 1.75
- key_up: bfloat16 [256, 1280], replicated, may hold values from -0.375 to 0.375
- value_up: bfloat16 [256, 1280], replicated, may hold values from -0.375 to 0.375
- output_weight: bfloat16 [1280, 2560], replicated, may hold values from -0.15625 to 0.15625
- post_gain: bfloat16 [2560], replicated, may hold values from 0.25 to 1.75
- gate_weight: bfloat16 [2560, 3200], P('tok', 'grp'), may hold values from -0.125 to 0.125
- up_weight: bfloat16 [2560, 3200], P('tok', 'grp'), may hold values from -0.125 to 0.125
- down_weight: bfloat16 [3200, 2560], P('grp', 'tok'), may hold values from -0.109375 to 0.109375
- cache_latents: bfloat16 [16, 4096, 288], P('grp', 'tok'), as said below
- prompt_latents: bfloat16 [8, 1024, 288], P(None, 'tok'), as said below
- cache_len: int32 [16], replicated, may hold values from 1 to 4096, 32768 in all
- prompt_len: int32 [8], replicated, may hold values from 1 to 1024, 4096 in all
- prompt_of: int32 [16], replicated, may hold values from 0 to 7
Outputs:
- layer_out: bfloat16 [16384, 2560], P(('grp', 'tok'))
- new_latents: bfloat16 [16384, 288], P(('grp', 'tok'))
Inputs may be any that keep to these rules, and one draw needn't show every extreme that they name: `cache_len`: some request has exactly 4096 live cached rows. `prompt_len`: some stored prompt has exactly 1024 live rows. `cache_latents`: rows past a request's live length are stored but never read. `prompt_latents`: rows past a prompt's live length are stored but never read.
All inputs are finite; a program needn't handle non-finite values.
Results may differ from a plain program's by a relative error of at most 0.02.
Values may be sent and summed in bfloat16 or wider, within the bound.
No kernel may reach another device: no remote copies, remote signals or barrier semaphores. Data moves between devices by JAX's collectives and lax.ppermute only.
A program may use at most 128 MiB of HBM per device.

v0:
```python
import jax
import jax.numpy as jnp
from jax import lax
from jax.sharding import PartitionSpec as P

KVR = 256
HEADS = 20
NOPE = 64
ROPE = 32
VDIM = 64
SPAN = 1024
EPSILON = 1e-06


def passed_along(block, axis, distance):
    devices = range(lax.axis_size(axis))
    route = [(i - distance, i) for i in devices if i - distance in devices]
    return lax.ppermute(block, axis, route)


def norm_rows(values, gain_vector):
    mean_square = jnp.mean(values * values, axis=-1, keepdims=True)
    return values * lax.rsqrt(mean_square + EPSILON) * gain_vector.astype(jnp.float32)


def rotate(values, positions):
    half_width = values.shape[-1] // 2
    frequency = 10000.0 ** (-jnp.arange(half_width, dtype=jnp.float32) / half_width)
    angles = positions.astype(jnp.float32)[:, None] * frequency[None, :]
    if values.ndim == 3:
        angles = angles[:, None, :]
    cosine = jnp.cos(angles)
    sine_part = jnp.sin(angles)
    leading = values[..., :half_width]
    trailing = values[..., half_width:]
    return jnp.concatenate(
        [leading * cosine - trailing * sine_part, trailing * cosine + leading * sine_part], axis=-1
    )


def attend_segment(
    softmax_state, queries, key_rows, lowers, limits, block_count, key_block, score_scale
):

    def fold_block(step_index, carried):
        running_max, running_sum, running_out = carried
        first_key = step_index * key_block
        key_piece = lax.dynamic_slice_in_dim(key_rows, first_key, key_block, 0)
        scores = (
            jnp.einsum("rw,kw->rk", queries, key_piece, preferred_element_type=jnp.float32)
            * score_scale
        )
        key_place = (first_key + jnp.arange(key_block, dtype=jnp.int32))[None, :]
        live_keys = jnp.logical_and(key_place >= lowers[:, None], key_place < limits[:, None])
        next_max = jnp.maximum(running_max, jnp.max(jnp.where(live_keys, scores, -1e30), axis=1))
        weights = jnp.where(live_keys, jnp.exp(scores - next_max[:, None]), 0.0)
        factor = jnp.exp(running_max - next_max)
        running_sum = running_sum * factor + jnp.sum(weights, axis=1)
        running_out = running_out * factor[:, None] + jnp.dot(
            weights.astype(jnp.bfloat16), key_piece[:, :KVR], preferred_element_type=jnp.float32
        )
        return (next_max, running_sum, running_out)

    return lax.fori_loop(0, block_count, fold_block, softmax_state)


def body(
    tokens,
    input_gain,
    query_down,
    query_gain,
    query_up,
    latent_down,
    latent_gain,
    key_up,
    value_up,
    output_weight,
    post_gain,
    gate_weight,
    up_weight,
    down_weight,
    cache_latents,
    prompt_latents,
    cache_len,
    prompt_len,
    prompt_of,
):
    group_index = lax.axis_index("grp")
    shard_index = lax.axis_index("tok")
    tok_dev = tokens.shape[0]
    tok_count = lax.axis_size("tok")
    group_requests = tok_dev * tok_count // SPAN
    local_request = shard_index % group_requests
    owner = group_index * group_requests + local_request
    offset = shard_index // group_requests * tok_dev
    within = offset + jnp.arange(tok_dev, dtype=jnp.int32)
    own_prompt = prompt_of[owner]
    prompt_live = prompt_len[own_prompt]
    cache_live = cache_len[owner]
    positions = prompt_live + cache_live + within
    normed = norm_rows(tokens.astype(jnp.float32), input_gain).astype(jnp.bfloat16)
    query_latent = norm_rows(
        jnp.dot(normed, query_down, preferred_element_type=jnp.float32), query_gain
    ).astype(jnp.bfloat16)
    query_full = jnp.dot(query_latent, query_up, preferred_element_type=jnp.float32).astype(
        jnp.bfloat16
    )
    query_full = lax.optimization_barrier(query_full).reshape(tok_dev, HEADS, NOPE + ROPE)
    absorbed = jnp.einsum(
        "thd,khd->thk",
        query_full[..., :NOPE],
        key_up.reshape(KVR, HEADS, NOPE),
        preferred_element_type=jnp.float32,
    )
    turned = rotate(query_full[..., NOPE:].astype(jnp.float32), positions)
    queries = jnp.concatenate([absorbed, turned], axis=-1).astype(jnp.bfloat16)
    latent_raw = jnp.dot(normed, latent_down, preferred_element_type=jnp.float32)
    new_latents = jnp.concatenate(
        [norm_rows(latent_raw[:, :KVR], latent_gain), rotate(latent_raw[:, KVR:], positions)],
        axis=-1,
    ).astype(jnp.bfloat16)
    latent_width = new_latents.shape[1]
    shards_back = SPAN // tok_dev
    earlier_pieces = []
    passing = new_latents
    for back in range(1, shards_back):
        passing = passed_along(passing, "tok", group_requests)
        earlier_pieces.insert(0, passing)
    span_rows = jnp.concatenate(earlier_pieces + [new_latents], axis=0)
    lead_rows = (shards_back - 1) * tok_dev
    span_lower = jnp.broadcast_to(lead_rows - offset, (tok_dev,))
    span_limit = lead_rows + 1 + jnp.arange(tok_dev, dtype=jnp.int32)
    cache_all, prompt_all = (
        lax.all_gather(cache_latents, "tok", axis=1, tiled=True),
        lax.all_gather(prompt_latents, "tok", axis=1, tiled=True),
    )
    cache_rows = lax.dynamic_index_in_dim(cache_all, local_request, 0, keepdims=False)
    prompt_rows = lax.dynamic_index_in_dim(prompt_all, own_prompt, 0, keepdims=False)
    query_rows = queries.reshape(tok_dev * HEADS, latent_width)
    row_count = tok_dev * HEADS
    score_scale = 1.0 / (NOPE + ROPE) ** 0.5
    softmax_state = (
        jnp.full((row_count,), -1e30, jnp.float32),
        jnp.zeros((row_count,), jnp.float32),
        jnp.zeros((row_count, KVR), jnp.float32),
    )
    no_lower = jnp.zeros((tok_dev,), jnp.int32)
    segments = (
        (prompt_rows, no_lower, jnp.broadcast_to(prompt_live, (tok_dev,))),
        (cache_rows, no_lower, jnp.broadcast_to(cache_live, (tok_dev,))),
        (span_rows, span_lower, span_limit),
    )
    for key_rows, token_lower, token_limit in segments:
        lowers = jnp.repeat(token_lower, HEADS)
        limits = jnp.repeat(token_limit, HEADS)
        key_block = min(512, key_rows.shape[0])
        block_count = key_rows.shape[0] // key_block
        softmax_state = attend_segment(
            softmax_state, query_rows, key_rows, lowers, limits, block_count, key_block, score_scale
        )
    running_max, running_sum, running_out = softmax_state
    latent_out = (
        (running_out / running_sum[:, None]).astype(jnp.bfloat16).reshape(tok_dev, HEADS, KVR)
    )
    heads_out = (
        jnp.einsum(
            "thk,khv->thv",
            latent_out,
            value_up.reshape(KVR, HEADS, VDIM),
            preferred_element_type=jnp.float32,
        )
        .astype(jnp.bfloat16)
        .reshape(tok_dev, HEADS * VDIM)
    )
    attended = jnp.dot(heads_out, output_weight, preferred_element_type=jnp.float32)
    residual = lax.optimization_barrier(
        (tokens.astype(jnp.float32) + attended).astype(jnp.bfloat16)
    )
    post_norm = norm_rows(residual.astype(jnp.float32), post_gain).astype(jnp.bfloat16)
    rows_all = lax.all_gather(post_norm, "grp", axis=0, tiled=True)
    gate_values = jnp.dot(
        rows_all,
        lax.all_gather(gate_weight, "tok", axis=0, tiled=True),
        preferred_element_type=jnp.float32,
    )
    up_values = jnp.dot(
        rows_all,
        lax.all_gather(up_weight, "tok", axis=0, tiled=True),
        preferred_element_type=jnp.float32,
    )
    hidden = (jax.nn.silu(gate_values) * up_values).astype(jnp.bfloat16)
    partial_out = jnp.dot(
        hidden,
        lax.all_gather(down_weight, "tok", axis=1, tiled=True),
        preferred_element_type=jnp.float32,
    )
    down_values = lax.psum_scatter(
        partial_out.astype(jnp.bfloat16), "grp", scatter_dimension=0, tiled=True
    ).astype(jnp.float32)
    layer_out = (residual.astype(jnp.float32) + down_values).astype(jnp.bfloat16)
    return (layer_out, new_latents)


def solution(mesh):
    in_specs = (
        P(("grp", "tok"), None),
        P(),
        P(),
        P(),
        P(),
        P(),
        P(),
        P(),
        P(),
        P(),
        P(),
        P("tok", "grp"),
        P("tok", "grp"),
        P("grp", "tok"),
        P("grp", "tok", None),
        P(None, "tok", None),
        P(),
        P(),
        P(),
    )
    out_specs = (P(("grp", "tok"), None), P(("grp", "tok"), None))
    return jax.shard_map(body, mesh=mesh, in_specs=in_specs, out_specs=out_specs, check_vma=False)
```

profile of v0, /device:TPU:1, one launch (start us, length us, event | category | flops | bytes accessed | tf_op | source)
XLA Modules:
  0.0 412.8 jit_solution(16430526760427926107)
XLA Ops:
  20.9 6.3 %collective-permute-start = (bf16[128,288]{0,1:T(8,128)(2,1)S(1)}, bf16[128,288]{0,1:T(8,128)(2,1)}, u32[]{:S(2)}, u32[]{:S(2)}) collective-permute-start(bf16[128,288]{0,1:T(8,128)(2,1)S(1)} %pad_maximum_fusion.1), channel_id=1, source_target_pairs={{0,4},{1,5},{2,6},{3,7},{4,8},{5,9},{6,10},{7,11},{8,12},{9,13},{1... | collective-permute-start | bytes 221192 | tf_op jit(solution)/shard_map/ppermute | solution.py:18
  27.2 3.2 multiply_reduce_fusion
  30.4 3.7 collective-permute-start.1
  36.4 4.5 %collective-permute-start.2 = (bf16[128,288]{0,1:T(8,128)(2,1)}, bf16[128,288]{0,1:T(8,128)(2,1)S(1)}, u32[]{:S(2)}, u32[]{:S(2)}) collective-permute-start(bf16[128,288]{0,1:T(8,128)(2,1)} %collective-permute-done.1), channel_id=1, source_target_pairs={{0,4},{1,5},{2,6},{3,7},{4,8},{5,9},{6,10},{7,11},{8,12},{9,13},{1... | collective-permute-start | bytes 221192 | tf_op jit(solution)/shard_map/ppermute | solution.py:18
  42.6 5.1 %collective-permute-start.3 = (bf16[128,288]{0,1:T(8,128)(2,1)S(1)}, bf16[128,288]{0,1:T(8,128)(2,1)S(1)}, u32[]{:S(2)}, u32[]{:S(2)}) collective-permute-start(bf16[128,288]{0,1:T(8,128)(2,1)S(1)} %collective-permute-done.2), channel_id=1, source_target_pairs={{0,4},{1,5},{2,6},{3,7},{4,8},{5,9},{6,10},{7,11},{8,12},{9,13},{1... | collective-permute-start | bytes 221192 | tf_op jit(solution)/shard_map/ppermute | solution.py:18
  47.7 2.9 collective-permute-done.3
  50.7 5.6 %collective-permute-start.4 = (bf16[128,288]{0,1:T(8,128)(2,1)S(1)}, bf16[128,288]{0,1:T(8,128)(2,1)S(1)}, u32[]{:S(2)}, u32[]{:S(2)}) collective-permute-start(bf16[128,288]{0,1:T(8,128)(2,1)S(1)} %collective-permute-done.3), channel_id=1, source_target_pairs={{0,4},{1,5},{2,6},{3,7},{4,8},{5,9},{6,10},{7,11},{8,12},{9,13},{1... | collective-permute-start | bytes 221192 | tf_op jit(solution)/shard_map/ppermute | solution.py:18
  62.0 6.0 %collective-permute-start.5 = (bf16[128,288]{0,1:T(8,128)(2,1)S(1)}, bf16[128,288]{0,1:T(8,128)(2,1)S(1)}, u32[]{:S(2)}, u32[]{:S(2)}) collective-permute-start(bf16[128,288]{0,1:T(8,128)(2,1)S(1)} %collective-permute-done.4), channel_id=1, source_target_pairs={{0,4},{1,5},{2,6},{3,7},{4,8},{5,9},{6,10},{7,11},{8,12},{9,13},{1... | collective-permute-start | bytes 221192 | tf_op jit(solution)/shard_map/ppermute | solution.py:18
  67.9 3.0 pad_maximum_fusion
  73.1 3.4 collective-permute-start.6
  87.5 26.8 %while.56 = (s32[]{:T(128)}, f32[2560]{0:T(1024)S(1)}, f32[2560]{0:T(1024)S(1)}, f32[2560,256]{1,0:T(8,128)S(1)}, bf16[1024,288]{1,0:T(8,128)(2,1)}, /*index=5*/...) while((s32[]{:T(128)}, f32[2560]{0:T(1024)S(1)}, ...), condition=%wide.region_5.6_spmd.clone, body=%wide.region_2.5_spmd.clone.sunk | while | flops 1439840768 | bytes 44730576 | solution.py:64
  88.0 5.6 %fusion.130 = (f32[2560]{0:T(1024)S(1)}, f32[512,2560]{1,0:T(8,128)}) fusion(pred[512]{0:T(512)(128)(4,1)S(1)} %fusion.129, bf16[2560,288]{1,0:T(8,128)(2,1)} %get-tuple-element.733, bf16[1024,288]{1,0:T(8,128)(2,1)} %get-tuple-element.732, s32[]{:T(128)S(6)} %select_n.152), kind=kOutput, calls=%fused_computation.53.clone.1 | convolution fusion | flops 758904320 | bytes 7612932 | tf_op jit(solution)/shard_map/while/body/eval_jaxpr/rw,kw->rk/dot_general | solution.py:50
  93.6 3.5 fusion.131
  97.7 2.9 convolution_add_fusion.9
  101.1 5.6 %fusion.130 = (f32[2560]{0:T(1024)S(1)}, f32[512,2560]{1,0:T(8,128)}) fusion(pred[512]{0:T(512)(128)(4,1)S(1)} %fusion.129, bf16[2560,288]{1,0:T(8,128)(2,1)} %get-tuple-element.733, bf16[1024,288]{1,0:T(8,128)(2,1)} %get-tuple-element.732, s32[]{:T(128)S(6)} %select_n.152), kind=kOutput, calls=%fused_computation.53.clone.1 | convolution fusion | flops 758904320 | bytes 7612932 | tf_op jit(solution)/shard_map/while/body/eval_jaxpr/rw,kw->rk/dot_general | solution.py:50
  106.8 3.5 fusion.131
  111.4 2.9 convolution_add_fusion.9
  114.3 14.3 %all-gather.9.cloned.1.call-done = bf16[4,4096,288]{1,2,0:T(8,128)(2,1)} async-done(((bf16[4,128,288]{1,2,0:T(8,128)(2,1)}), bf16[4,4096,288]{1,2,0:T(8,128)(2,1)}) %all-gather.9.cloned.1.call-update) | async-done | bytes 9437200 | tf_op jit(solution)/shard_map/all_gather | solution.py:134
  128.6 3.3 constant_dynamic-slice_fusion
  131.9 4.5 %copy.36 = bf16[1,4096,288]{2,1,0:T(8,128)(2,1)} copy(bf16[1,4096,288]{1,2,0:T(8,128)(2,1)} %constant_dynamic-slice_fusion) | data formatting | bytes 4718592 | tf_op jit(solution)/shard_map/jit(dynamic_index_in_dim)/dynamic_slice | solution.py:137
  136.4 61.9 %while.54 = (s32[]{:T(128)}, f32[2560]{0:T(1024)S(1)}, f32[2560]{0:T(1024)S(1)}, f32[2560,256]{1,0:T(8,128)S(1)}, bf16[4096,288]{1,0:T(8,128)(2,1)}, /*index=5*/...) while((s32[]{:T(128)}, f32[2560]{0:T(1024)S(1)}, ...), condition=%wide.region_9.10_spmd.clone, body=%wide.region_6.9_spmd.clone.sunk | while | flops 1439177728 | bytes 23759020 | solution.py:64
  137.0 3.3 fusion.119
  141.4 2.7 convolution_add_fusion.7
  144.7 3.3 fusion.119
  149.1 2.7 convolution_add_fusion.7
  152.5 3.3 fusion.119
  156.9 2.7 convolution_add_fusion.7
  160.2 3.3 fusion.119
  164.6 2.7 convolution_add_fusion.7
  167.9 3.4 fusion.119
  172.4 2.7 convolution_add_fusion.7
  175.7 3.3 fusion.119
  180.1 2.7 convolution_add_fusion.7
  183.5 3.3 fusion.119
  187.8 2.7 convolution_add_fusion.7
  191.2 3.3 fusion.119
  198.3 19.1 %while.55 = (s32[]{:T(128)}, f32[2560]{0:T(1024)S(1)}, f32[2560]{0:T(1024)S(1)}, f32[2560,256]{1,0:T(8,128)S(1)}, bf16[1024,288]{0,1:T(8,128)(2,1)}, /*index=5*/...) while((s32[]{:T(128)}, f32[2560]{0:T(1024)S(1)}, ...), condition=%wide.region_14.15_spmd.clone, body=%wide.region_11.14_spmd.clone.sunk | while | flops 1447041536 | bytes 23730872 | solution.py:64
  198.7 4.0 fusion.124
  204.6 3.3 convolution_add_fusion.8
  208.2 4.0 fusion.124
  214.1 3.3 convolution_add_fusion.8
  221.9 3.9 fusion.59
  228.6 32.8 %all-gather.11.cloned.1.call-done = bf16[512,2560]{1,0:T(8,128)(2,1)} async-done(((bf16[128,2560]{1,0:T(8,128)(2,1)}), bf16[512,2560]{1,0:T(8,128)(2,1)}) %all-gather.11.cloned.1.call-update) | async-done | bytes 2621456 | tf_op jit(solution)/shard_map/all_gather | solution.py:180
  261.4 6.7 %fusion.81 = f32[512,800]{0,1:T(8,128)} fusion(bf16[512,2560]{1,0:T(8,128)(2,1)} %all-gather.11.cloned.1.call-done, bf16[2560,800]{1,0:T(8,128)(2,1)} %all-gather.13.cloned.1.call-done), kind=kOutput, calls=%fused_computation.136 | convolution fusion | flops 2097152000 | bytes 8355840 | tf_op jit(solution)/shard_map/dot_general | solution.py:181
  268.1 42.8 %all-gather.15.cloned.1.call-done = bf16[2560,800]{1,0:T(8,128)(2,1)} async-done(((bf16[80,800]{1,0:T(8,128)(2,1)}), bf16[2560,800]{1,0:T(8,128)(2,1)}) %all-gather.15.cloned.1.call-update) | async-done | bytes 4096016 | tf_op jit(solution)/shard_map/all_gather | solution.py:188
  310.9 48.1 %all-gather.17.cloned.1.call-done = bf16[800,2560]{0,1:T(8,128)(2,1)} async-done(((bf16[800,80]{0,1:T(8,128)(2,1)}), bf16[800,2560]{0,1:T(8,128)(2,1)}) %all-gather.17.cloned.1.call-update) | async-done | bytes 4096016 | tf_op jit(solution)/shard_map/all_gather | solution.py:194
  358.9 11.8 %convolution_convert_fusion = bf16[512,2560]{1,0:T(8,128)(2,1)} fusion(bf16[800,2560]{0,1:T(8,128)(2,1)} %all-gather.17.cloned.1.call-done, f32[512,800]{0,1:T(8,128)} %fusion.81, bf16[512,2560]{1,0:T(8,128)(2,1)} %all-gather.11.cloned.1.call-done, bf16[2560,800]{1,0:T(8,128)(2,1)} %all-gather.15.cloned.1.call-done), kind=kOutput, calls=%fused_computation.77 | convolution fusion | flops 4198072320 | bytes 15073280 | tf_op jit(solution)/shard_map/dot_general | solution.py:192
  370.7 32.9 %reduce-scatter.2.cloned.1.call-done = bf16[128,2560]{1,0:T(8,128)(2,1)} async-done(((bf16[512,2560]{1,0:T(8,128)(2,1)}), bf16[128,2560]{1,0:T(8,128)(2,1)}) %reduce-scatter.2.cloned.1.call-update) | async-done | bytes 655376 | tf_op jit(solution)/shard_map/reduce_scatter | solution.py:197
  (160 shorter events, 65.5 us)
Async XLA Ops:
  7.2 26.9 %copy-start = (bf16[768,1920]{1,0:T(8,128)(2,1)S(1)}, bf16[768,1920]{1,0:T(8,128)(2,1)}, u32[]{:S(2)}) copy-start(bf16[768,1920]{1,0:T(8,128)(2,1)} %param.29) | copy-start | bytes 8847364
  7.2 78.2 %all-gather.7.cloned.1.call-start = ((), (), s32[]{:S(2)}) async-start(), calls=%async_computation.1 | async-start | bytes 6488064 | tf_op jit(solution)/shard_map/all_gather | solution.py:135
  7.9 120.7 %all-gather.9.cloned.1.call-start = ((), (), s32[]{:S(2)}) async-start(), calls=%async_computation.2 | async-start | bytes 9732096 | tf_op jit(solution)/shard_map/all_gather | solution.py:134
  8.7 219.9 %all-gather.13.cloned.1.call-start = ((), (), s32[]{:S(2)}) async-start(), calls=%async_computation.4 | async-start | bytes 4730880 | tf_op jit(solution)/shard_map/all_gather | solution.py:183
  20.8 9.6 %copy-start.8 = (bf16[768]{0:T(1024)(128)(2,1)S(1)}, bf16[768]{0:T(1024)(128)(2,1)}, u32[]{:S(2)}) copy-start(bf16[768]{0:T(1024)(128)(2,1)} %param.28) | copy-start | bytes 4612
  20.8 13.3 %copy-start.6 = (bf16[128,288]{0,1:T(8,128)(2,1)}, bf16[128,288]{0,1:T(8,128)(2,1)S(1)}, u32[]{:S(2)}) copy-start(bf16[128,288]{0,1:T(8,128)(2,1)S(1)} %pad_maximum_fusion.1) | copy-start | bytes 221188
  20.9 9.6 %collective-permute-start = (bf16[128,288]{0,1:T(8,128)(2,1)S(1)}, bf16[128,288]{0,1:T(8,128)(2,1)}, u32[]{:S(2)}, u32[]{:S(2)}) collective-permute-start(bf16[128,288]{0,1:T(8,128)(2,1)S(1)} %pad_maximum_fusion.1), channel_id=1, source_target_pairs={{0,4},{1,5},{2,6},{3,7},{4,8},{5,9},{6,10},{7,11},{8,12},{9,13},{1... | collective-permute-start | bytes 221192 | tf_op jit(solution)/shard_map/ppermute | solution.py:18
  27.1 234.2 %all-gather.11.cloned.1.call-start = ((), (), s32[]{:S(2)}) async-start(), calls=%async_computation.3 | async-start | bytes 3276800 | tf_op jit(solution)/shard_map/all_gather | solution.py:180
  30.4 5.9 %collective-permute-start.1 = (bf16[128,288]{0,1:T(8,128)(2,1)}, bf16[128,288]{0,1:T(8,128)(2,1)}, u32[]{:S(2)}, u32[]{:S(2)}) collective-permute-start(bf16[128,288]{0,1:T(8,128)(2,1)} %collective-permute-done), channel_id=1, source_target_pairs={{0,4},{1,5},{2,6},{3,7},{4,8},{5,9},{6,10},{7,11},{8,12},{9,13},{1... | collective-permute-start | bytes 221192 | tf_op jit(solution)/shard_map/ppermute | solution.py:18
  36.4 6.2 %collective-permute-start.2 = (bf16[128,288]{0,1:T(8,128)(2,1)}, bf16[128,288]{0,1:T(8,128)(2,1)S(1)}, u32[]{:S(2)}, u32[]{:S(2)}) collective-permute-start(bf16[128,288]{0,1:T(8,128)(2,1)} %collective-permute-done.1), channel_id=1, source_target_pairs={{0,4},{1,5},{2,6},{3,7},{4,8},{5,9},{6,10},{7,11},{8,12},{9,13},{1... | collective-permute-start | bytes 221192 | tf_op jit(solution)/shard_map/ppermute | solution.py:18
  42.6 8.1 %collective-permute-start.3 = (bf16[128,288]{0,1:T(8,128)(2,1)S(1)}, bf16[128,288]{0,1:T(8,128)(2,1)S(1)}, u32[]{:S(2)}, u32[]{:S(2)}) collective-permute-start(bf16[128,288]{0,1:T(8,128)(2,1)S(1)} %collective-permute-done.2), channel_id=1, source_target_pairs={{0,4},{1,5},{2,6},{3,7},{4,8},{5,9},{6,10},{7,11},{8,12},{9,13},{1... | collective-permute-start | bytes 221192 | tf_op jit(solution)/shard_map/ppermute | solution.py:18
  50.7 11.3 %collective-permute-start.4 = (bf16[128,288]{0,1:T(8,128)(2,1)S(1)}, bf16[128,288]{0,1:T(8,128)(2,1)S(1)}, u32[]{:S(2)}, u32[]{:S(2)}) collective-permute-start(bf16[128,288]{0,1:T(8,128)(2,1)S(1)} %collective-permute-done.3), channel_id=1, source_target_pairs={{0,4},{1,5},{2,6},{3,7},{4,8},{5,9},{6,10},{7,11},{8,12},{9,13},{1... | collective-permute-start | bytes 221192 | tf_op jit(solution)/shard_map/ppermute | solution.py:18
  62.0 11.2 %copy-start.7 = (bf16[2560]{0:T(1024)(128)(2,1)S(1)}, bf16[2560]{0:T(1024)(128)(2,1)}, u32[]{:S(2)}) copy-start(bf16[2560]{0:T(1024)(128)(2,1)} %param.35) | copy-start | bytes 15364
  62.0 11.2 %collective-permute-start.5 = (bf16[128,288]{0,1:T(8,128)(2,1)S(1)}, bf16[128,288]{0,1:T(8,128)(2,1)S(1)}, u32[]{:S(2)}, u32[]{:S(2)}) collective-permute-start(bf16[128,288]{0,1:T(8,128)(2,1)S(1)} %collective-permute-done.4), channel_id=1, source_target_pairs={{0,4},{1,5},{2,6},{3,7},{4,8},{5,9},{6,10},{7,11},{8,12},{9,13},{1... | collective-permute-start | bytes 221192 | tf_op jit(solution)/shard_map/ppermute | solution.py:18
  73.1 5.2 %collective-permute-start.6 = (bf16[128,288]{0,1:T(8,128)(2,1)S(1)}, bf16[128,288]{0,1:T(8,128)(2,1)S(1)}, u32[]{:S(2)}, u32[]{:S(2)}) collective-permute-start(bf16[128,288]{0,1:T(8,128)(2,1)S(1)} %collective-permute-done.5), channel_id=1, source_target_pairs={{0,4},{1,5},{2,6},{3,7},{4,8},{5,9},{6,10},{7,11},{8,12},{9,13},{1... | collective-permute-start | bytes 221192 | tf_op jit(solution)/shard_map/ppermute | solution.py:18
  93.6 4.0 copy-start.2
  106.8 4.7 %copy-start.2 = (f32[512,2560]{1,0:T(8,128)S(1)}, f32[512,2560]{1,0:T(8,128)}, u32[]{:S(2)}) copy-start(f32[512,2560]{1,0:T(8,128)} %get-tuple-element.703) | copy-start | bytes 15728644 | tf_op jit(solution)/shard_map/while
  218.9 2.3 copy-start.5
  218.9 2.9 copy-start.4
  225.8 42.3 %copy-start.3 = (bf16[128,2560]{1,0:T(8,128)(2,1)}, bf16[128,2560]{1,0:T(8,128)(2,1)S(1)}, u32[]{:S(2)}) copy-start(bf16[128,2560]{1,0:T(8,128)(2,1)S(1)} %fusion.59) | copy-start | bytes 1966084
  227.1 83.7 %all-gather.15.cloned.1.call-start = ((), (), s32[]{:S(2)}) async-start(), calls=%async_computation.5 | async-start | bytes 4730880 | tf_op jit(solution)/shard_map/all_gather | solution.py:188
  227.7 131.2 %all-gather.17.cloned.1.call-start = ((), (), s32[]{:S(2)}) async-start(), calls=%async_computation.6 | async-start | bytes 4730880 | tf_op jit(solution)/shard_map/all_gather | solution.py:194
  228.3 175.4 %reduce-scatter.2.cloned.1.call-start = ((), (), s32[]{:S(2)}) async-start(), calls=%async_computation.7 | async-start | bytes 3276800 | tf_op jit(solution)/shard_map/reduce_scatter | solution.py:197
  358.9 47.0 %copy-start.1 = (bf16[768,1920]{1,0:T(8,128)(2,1)S(1)}, bf16[768,1920]{1,0:T(8,128)(2,1)}, u32[]{:S(2)}) copy-start(bf16[768,1920]{1,0:T(8,128)(2,1)} %param.29) | copy-start | bytes 8847364
Sparse Core Ops, SparseCore 0:
  10.3 55.2 all-gather.6
  67.7 60.8 all-gather.8
  130.9 46.1 all-gather.12
  227.2 34.1 all-gather.10
  263.6 47.2 all-gather.14
  313.0 45.8 all-gather.16
  370.9 32.7 reduce-scatter.1
where the time goes:
time: 415 us; the launch traced here: 413 us
  waiting for transfers between devices  179 us (43%)
  matrix products  109 us (26%)
  other arithmetic  37.2 us (9%)
  starting transfers between devices  35.1 us (8%)
  local copies, waits for them, and re-layouts  33.7 us (8%)
  between operations  17.6 us (4%)
    all_gather x1, waiting for transfers between devices, body(): lax.all_gather(down_weight, 'tok', axis=1, tiled=True)  48.1 us
    dot_general x12, matrix products, fold_block(): jnp.einsum('rw,kw->rk', queries, key_piece, preferred_element_type=jnp.fl...  45.9 us
    all_gather x1, waiting for transfers between devices, body(): lax.all_gather(up_weight, 'tok', axis=0, tiled=True)  42.8 us
    ppermute x7, starting transfers between devices, passed_along(): return lax.ppermute(block, axis, route)  34.6 us
    dot_general x12, matrix products, fold_block(): jnp.dot(weights.astype(jnp.bfloat16), key_piece[:, :KVR], preferred_eleme...  33.7 us
    reduce_scatter x1, waiting for transfers between devices, body(): lax.psum_scatter(partial_out.astype(jnp.bfloat16), 'grp', scatter_dimensi...  32.9 us
    all_gather x1, waiting for transfers between devices, body(): rows_all = lax.all_gather(post_norm, 'grp', axis=0, tiled=True)  32.8 us
    reduce_sum x12, other arithmetic, fold_block(): running_sum = running_sum * factor + jnp.sum(weights, axis=1)  19 us
  transfers between devices with their start and end apart: 14, of which 8 were waited for; matrix products, arithmetic and copies ran while one was open for 40% of the time, Pallas kernels for 0%

commit v1 on v0

--- a/solution.py
+++ b/solution.py
@@ -10,6 +10,11 @@
 VDIM = 64
 SPAN = 1024
 EPSILON = 1e-06
+
+
+def tiled_gather(array, axis, dim):
+    copies = jnp.concatenate([array] * lax.axis_size(axis), axis=dim)
+    return lax.all_to_all(copies, axis, dim, dim, tiled=True)
 
 
 def passed_along(block, axis, distance):
@@ -131,7 +136,7 @@
     span_lower = jnp.broadcast_to(lead_rows - offset, (tok_dev,))
     span_limit = lead_rows + 1 + jnp.arange(tok_dev, dtype=jnp.int32)
     cache_all, prompt_all = (
-        lax.all_gather(cache_latents, "tok", axis=1, tiled=True),
+        tiled_gather(cache_latents, "tok", 1),
         lax.all_gather(prompt_latents, "tok", axis=1, tiled=True),
     )
     cache_rows = lax.dynamic_index_in_dim(cache_all, local_request, 0, keepdims=False)

time: 415 us -> 633 us (1.53)
  waiting for transfers between devices: 179 us -> 306 us
  local copies, waits for them, and re-layouts: 33.7 us -> 99.9 us
  starting transfers between devices: 35.1 us -> 58.8 us
    ppermute x7, waiting for transfers between devices: 5.92 us -> 139 us  [passed_along(): return lax.ppermute(block, axis, route)]
    unnamed x25 -> x65, local copies, waits for them, and re-layouts: 9.84 us -> 56.6 us
    concatenate x0 -> x2, local copies, waits for them, and re-layouts: none -> 20 us  [tiled_gather(): copies = jnp.concatenate([array] * lax.axis_size(axis), axis=dim)]
    all_gather x1 -> x0, waiting for transfers between devices: 14.3 us -> none  [body(): lax.all_gather(cache_latents, 'tok', axis=1, tiled=True)]
    ppermute x7, starting transfers between devices: 34.6 us -> 48.5 us  [passed_along(): return lax.ppermute(block, axis, route)]
    all_to_all x0 -> x1, starting transfers between devices: none -> 9.8 us  [tiled_gather(): return lax.all_to_all(copies, axis, dim, dim, tiled=True)]
    all_gather x1, waiting for transfers between devices: 32.8 us -> 40.8 us  [body(): rows_all = lax.all_gather(post_norm, 'grp', axis=0, tiled=True)]
  transfers between devices with their start and end apart: 14 -> 14, of which waited for: 8 -> 8; matrix products, arithmetic and copies ran while one was open for 40% -> 37% of each run, Pallas kernels for 0% -> 0%
where the time goes in v1:
time: 633 us; the launch traced here: 630 us
  waiting for transfers between devices  306 us (48%)
  matrix products  112 us (18%)
  local copies, waits for them, and re-layouts  99.9 us (16%)
  starting transfers between devices  58.8 us (9%)
  other arithmetic  35.3 us (6%)
  between operations  17.6 us (3%)
    ppermute x7, waiting for transfers between devices, passed_along(): return lax.ppermute(block, axis, route)  139 us
    unnamed x65, local copies, waits for them, and re-layouts  56.6 us
    ppermute x7, starting transfers between devices, passed_along(): return lax.ppermute(block, axis, route)  48.5 us
    all_gather x1, waiting for transfers between devices, body(): lax.all_gather(down_weight, 'tok', axis=1, tiled=True)  48 us
    dot_general x12, matrix products, fold_block(): jnp.einsum('rw,kw->rk', queries, key_piece, preferred_element_type=jnp.fl...  47.2 us
    all_gather x1, waiting for transfers between devices, body(): lax.all_gather(up_weight, 'tok', axis=0, tiled=True)  42.8 us
    all_gather x1, waiting for transfers between devices, body(): rows_all = lax.all_gather(post_norm, 'grp', axis=0, tiled=True)  40.8 us
    dot_general x12, matrix products, fold_block(): jnp.dot(weights.astype(jnp.bfloat16), key_piece[:, :KVR], preferred_eleme...  33.7 us
  transfers between devices with their start and end apart: 14, of which 8 were waited for; matrix products, arithmetic and copies ran while one was open for 37% of the time, Pallas kernels for 0%

profile of v1, /device:TPU:1, one launch (start us, length us, event | category | flops | bytes accessed | tf_op | source)
XLA Modules:
  0.0 630.0 jit_solution(3551513141823834616)
XLA Ops:
  41.6 19.2 %copy.133 = bf16[4,4096,288]{2,0,1:T(4,128)(2,1)} copy(bf16[4,4096,288]{1,2,0:T(8,128)(2,1)} %constant_dynamic-update-slice_fusion) | data formatting | bytes 18874368 | tf_op jit(solution)/shard_map/concatenate | solution.py:16
  60.8 9.8 %all-to-all-start = ((bf16[4,4096,288]{2,0,1:T(4,128)(2,1)}), bf16[4,4096,288]{2,0,1:T(4,128)(2,1)}, u32[]{:S(2)}, u32[]{:S(2)}) async-start(bf16[4,4096,288]{2,0,1:T(4,128)(2,1)} %copy.133), calls=%async_computation | async-start | bytes 25165824 | tf_op jit(solution)/shard_map/all_to_all | solution.py:17
  79.5 5.4 collective-permute-start
  85.0 3.1 multiply_reduce_fusion
  88.1 135.7 %collective-permute-done = bf16[128,288]{0,1:T(8,128)(2,1)} collective-permute-done((bf16[128,288]{0,1:T(8,128)(2,1)S(1)}, bf16[128,288]{0,1:T(8,128)(2,1)}, u32[]{:S(2)}, u32[]{:S(2)}) %collective-permute-start) | collective-permute-done | bytes 73760 | tf_op jit(solution)/shard_map/ppermute | solution.py:23
  223.9 10.0 %collective-permute-start.1 = (bf16[128,288]{0,1:T(8,128)(2,1)}, bf16[128,288]{0,1:T(8,128)(2,1)}, u32[]{:S(2)}, u32[]{:S(2)}) collective-permute-start(bf16[128,288]{0,1:T(8,128)(2,1)} %collective-permute-done), channel_id=1, source_target_pairs={{0,4},{1,5},{2,6},{3,7},{4,8},{5,9},{6,10},{7,11},{8,12},{9,13},{1... | collective-permute-start | bytes 221192 | tf_op jit(solution)/shard_map/ppermute | solution.py:23
  236.1 6.0 collective-permute-start.2
  243.9 8.8 %collective-permute-start.3 = (bf16[128,288]{0,1:T(8,128)(2,1)S(1)}, bf16[128,288]{0,1:T(8,128)(2,1)S(1)}, u32[]{:S(2)}, u32[]{:S(2)}) collective-permute-start(bf16[128,288]{0,1:T(8,128)(2,1)S(1)} %collective-permute-done.2), channel_id=1, source_target_pairs={{0,4},{1,5},{2,6},{3,7},{4,8},{5,9},{6,10},{7,11},{8,12},{9,13},{1... | collective-permute-start | bytes 221192 | tf_op jit(solution)/shard_map/ppermute | solution.py:23
  254.1 6.6 %collective-permute-start.4 = (bf16[128,288]{0,1:T(8,128)(2,1)S(1)}, bf16[128,288]{0,1:T(8,128)(2,1)S(1)}, u32[]{:S(2)}, u32[]{:S(2)}) collective-permute-start(bf16[128,288]{0,1:T(8,128)(2,1)S(1)} %collective-permute-done.3), channel_id=1, source_target_pairs={{0,4},{1,5},{2,6},{3,7},{4,8},{5,9},{6,10},{7,11},{8,12},{9,13},{1... | collective-permute-start | bytes 221192 | tf_op jit(solution)/shard_map/ppermute | solution.py:23
  266.3 6.1 collective-permute-start.5
  272.5 3.0 pad_maximum_fusion
  277.6 5.6 collective-permute-start.6
  291.4 10.1 %constant_dynamic-slice_fusion = bf16[1,4096,288]{2,0,1:T(2,128)(2,1)} fusion(bf16[4,4096,288]{2,0,1:T(4,128)(2,1)} %all-to-all-done, s32[]{:T(128)S(6)} %select_n.92), kind=kLoop, calls=%fused_computation.166 | loop fusion | bytes 4718596 | tf_op jit(solution)/shard_map/jit(dynamic_index_in_dim)/dynamic_slice | solution.py:142
  301.5 13.9 %copy.141 = bf16[1,4096,288]{1,2,0:T(8,128)(2,1)} copy(bf16[1,4096,288]{2,0,1:T(2,128)(2,1)} %constant_dynamic-slice_fusion) | data formatting | bytes 4718592
  317.4 26.3 %while.56 = (s32[]{:T(128)}, f32[2560]{0:T(1024)S(1)}, f32[2560]{0:T(1024)S(1)}, f32[2560,256]{1,0:T(8,128)S(1)}, bf16[1024,288]{1,0:T(8,128)(2,1)}, /*index=5*/...) while((s32[]{:T(128)}, f32[2560]{0:T(1024)S(1)}, ...), condition=%wide.region_5.6_spmd.clone, body=%wide.region_2.5_spmd.clone.sunk | while | flops 1439840768 | bytes 44730576 | solution.py:69
  318.1 5.6 fusion.130
  323.7 3.5 fusion.131
  327.7 2.9 convolution_add_fusion.9
  331.2 5.6 fusion.130
  336.9 3.5 fusion.131
  340.9 2.9 convolution_add_fusion.9
  343.8 62.6 %while.54 = (s32[]{:T(128)}, f32[2560]{0:T(1024)S(1)}, f32[2560]{0:T(1024)S(1)}, f32[2560,256]{1,0:T(8,128)S(1)}, bf16[4096,288]{0,1:T(8,128)(2,1)}, /*index=5*/...) while((s32[]{:T(128)}, f32[2560]{0:T(1024)S(1)}, ...), condition=%wide.region_9.10_spmd.clone, body=%wide.region_6.9_spmd.clone.sunk | while | flops 1439177728 | bytes 23660716 | solution.py:69
  344.3 3.5 fusion.119
  352.2 3.5 fusion.119
  356.7 2.7 convolution_add_fusion.7
  360.0 3.5 fusion.119
  364.5 2.7 convolution_add_fusion.7
  367.8 3.5 fusion.119
  372.4 2.7 convolution_add_fusion.7
  375.6 3.5 fusion.119
  383.5 3.5 fusion.119
  388.0 2.7 convolution_add_fusion.7
  391.3 3.5 fusion.119
  395.8 2.7 convolution_add_fusion.7
  399.1 3.5 fusion.119
  403.7 2.7 convolution_add_fusion.7
  406.4 19.1 %while.55 = (s32[]{:T(128)}, f32[2560]{0:T(1024)S(1)}, f32[2560]{0:T(1024)S(1)}, f32[2560,256]{1,0:T(8,128)S(1)}, bf16[1024,288]{0,1:T(8,128)(2,1)}, /*index=5*/...) while((s32[]{:T(128)}, f32[2560]{0:T(1024)S(1)}, ...), condition=%wide.region_14.15_spmd.clone, body=%wide.region_11.14_spmd.clone.sunk | while | flops 1447041536 | bytes 23730872 | solution.py:69
  406.8 4.0 fusion.124
  412.7 3.3 convolution_add_fusion.8
  416.3 4.0 fusion.124
  422.2 3.3 convolution_add_fusion.8
  430.9 4.0 fusion.59
  437.8 40.8 %all-gather.8.cloned.1.call-done = bf16[512,2560]{1,0:T(8,128)(2,1)} async-done(((bf16[128,2560]{1,0:T(8,128)(2,1)}), bf16[512,2560]{1,0:T(8,128)(2,1)}) %all-gather.8.cloned.1.call-update) | async-done | bytes 2621456 | tf_op jit(solution)/shard_map/all_gather | solution.py:185
  478.5 6.7 %fusion.81 = f32[512,800]{0,1:T(8,128)} fusion(bf16[512,2560]{1,0:T(8,128)(2,1)} %all-gather.8.cloned.1.call-done, bf16[2560,800]{1,0:T(8,128)(2,1)} %all-gather.10.cloned.1.call-done), kind=kOutput, calls=%fused_computation.168 | convolution fusion | flops 2097152000 | bytes 8355840 | tf_op jit(solution)/shard_map/dot_general | solution.py:186
  485.2 42.8 %all-gather.12.cloned.1.call-done = bf16[2560,800]{1,0:T(8,128)(2,1)} async-done(((bf16[80,800]{1,0:T(8,128)(2,1)}), bf16[2560,800]{1,0:T(8,128)(2,1)}) %all-gather.12.cloned.1.call-update) | async-done | bytes 4096016 | tf_op jit(solution)/shard_map/all_gather | solution.py:193
  528.0 48.0 %all-gather.14.cloned.1.call-done = bf16[800,2560]{0,1:T(8,128)(2,1)} async-done(((bf16[800,80]{0,1:T(8,128)(2,1)}), bf16[800,2560]{0,1:T(8,128)(2,1)}) %all-gather.14.cloned.1.call-update) | async-done | bytes 4096016 | tf_op jit(solution)/shard_map/all_gather | solution.py:199
  576.0 11.8 %convolution_convert_fusion = bf16[512,2560]{1,0:T(8,128)(2,1)} fusion(bf16[800,2560]{0,1:T(8,128)(2,1)} %all-gather.14.cloned.1.call-done, f32[512,800]{0,1:T(8,128)} %fusion.81, bf16[512,2560]{1,0:T(8,128)(2,1)} %all-gather.8.cloned.1.call-done, bf16[2560,800]{1,0:T(8,128)(2,1)} %all-gather.12.cloned.1.call-done), kind=kOutput, calls=%fused_computation.77 | convolution fusion | flops 4198072320 | bytes 15073280 | tf_op jit(solution)/shard_map/dot_general | solution.py:197
  587.9 32.9 %reduce-scatter.2.cloned.1.call-done = bf16[128,2560]{1,0:T(8,128)(2,1)} async-done(((bf16[512,2560]{1,0:T(8,128)(2,1)}), bf16[128,2560]{1,0:T(8,128)(2,1)}) %reduce-scatter.2.cloned.1.call-update) | async-done | bytes 655376 | tf_op jit(solution)/shard_map/reduce_scatter | solution.py:202
  (200 shorter events, 98.3 us)
Async XLA Ops:
  7.2 226.7 %copy-start = (bf16[768,1920]{1,0:T(8,128)(2,1)S(1)}, bf16[768,1920]{1,0:T(8,128)(2,1)}, u32[]{:S(2)}) copy-start(bf16[768,1920]{1,0:T(8,128)(2,1)} %param.29) | copy-start | bytes 8847364
  7.2 16.5 %copy-start.2 = (bf16[4,128,288]{1,2,0:T(8,128)(2,1)S(1)}, bf16[4,128,288]{1,2,0:T(8,128)(2,1)}, u32[]{:S(2)}) copy-start(bf16[4,128,288]{1,2,0:T(8,128)(2,1)} %param.39) | copy-start | bytes 884740
  7.2 308.1 %all-gather.6.cloned.1.call-start = ((), (), s32[]{:S(2)}) async-start(), calls=%async_computation.2 | async-start | bytes 6488064 | tf_op jit(solution)/shard_map/all_gather | solution.py:140
  60.8 9.9 %copy-start.9 = (s32[16]{0:T(128)S(1)}, s32[16]{0:T(128)}, u32[]{:S(2)}) copy-start(s32[16]{0:T(128)} %param.43) | copy-start | bytes 196
  60.8 11.8 %copy-start.10 = (s32[16]{0:T(128)S(1)}, s32[16]{0:T(128)}, u32[]{:S(2)}) copy-start(s32[16]{0:T(128)} %param.41) | copy-start | bytes 196
  60.8 12.4 %copy-start.6 = (bf16[2560]{0:T(1024)(128)(2,1)S(1)}, bf16[2560]{0:T(1024)(128)(2,1)}, u32[]{:S(2)}) copy-start(bf16[2560]{0:T(1024)(128)(2,1)} %param.26) | copy-start | bytes 15364
  60.8 12.4 %copy-start.11 = (bf16[256]{0:T(256)(128)(2,1)S(1)}, bf16[256]{0:T(256)(128)(2,1)}, u32[]{:S(2)}) copy-start(bf16[256]{0:T(256)(128)(2,1)} %param.31) | copy-start | bytes 1540
  60.8 13.0 %copy-start.12 = (s32[8]{0:T(128)S(1)}, s32[8]{0:T(128)}, u32[]{:S(2)}) copy-start(s32[8]{0:T(128)} %param.42) | copy-start | bytes 100
  60.8 230.6 %all-to-all-start = ((bf16[4,4096,288]{2,0,1:T(4,128)(2,1)}), bf16[4,4096,288]{2,0,1:T(4,128)(2,1)}, u32[]{:S(2)}, u32[]{:S(2)}) async-start(bf16[4,4096,288]{2,0,1:T(4,128)(2,1)} %copy.133), calls=%async_computation | async-start | bytes 25165824 | tf_op jit(solution)/shard_map/all_to_all | solution.py:17
  70.6 17.5 %copy-start.8 = (bf16[768]{0:T(1024)(128)(2,1)S(1)}, bf16[768]{0:T(1024)(128)(2,1)}, u32[]{:S(2)}) copy-start(bf16[768]{0:T(1024)(128)(2,1)} %param.28) | copy-start | bytes 4612
  70.6 367.1 %all-gather.10.cloned.1.call-start = ((), (), s32[]{:S(2)}) async-start(), calls=%async_computation.4 | async-start | bytes 4730880 | tf_op jit(solution)/shard_map/all_gather | solution.py:188
  79.5 154.4 %copy-start.5 = (bf16[128,288]{0,1:T(8,128)(2,1)}, bf16[128,288]{0,1:T(8,128)(2,1)S(1)}, u32[]{:S(2)}) copy-start(bf16[128,288]{0,1:T(8,128)(2,1)S(1)} %pad_maximum_fusion.1) | copy-start | bytes 221188
  79.5 144.4 %collective-permute-start = (bf16[128,288]{0,1:T(8,128)(2,1)S(1)}, bf16[128,288]{0,1:T(8,128)(2,1)}, u32[]{:S(2)}, u32[]{:S(2)}) collective-permute-start(bf16[128,288]{0,1:T(8,128)(2,1)S(1)} %pad_maximum_fusion.1), channel_id=1, source_target_pairs={{0,4},{1,5},{2,6},{3,7},{4,8},{5,9},{6,10},{7,11},{8,12},{9,13},{1... | collective-permute-start | bytes 221192 | tf_op jit(solution)/shard_map/ppermute | solution.py:23
  84.9 393.6 %all-gather.8.cloned.1.call-start = ((), (), s32[]{:S(2)}) async-start(), calls=%async_computation.3 | async-start | bytes 3276800 | tf_op jit(solution)/shard_map/all_gather | solution.py:185
  223.9 12.3 %collective-permute-start.1 = (bf16[128,288]{0,1:T(8,128)(2,1)}, bf16[128,288]{0,1:T(8,128)(2,1)}, u32[]{:S(2)}, u32[]{:S(2)}) collective-permute-start(bf16[128,288]{0,1:T(8,128)(2,1)} %collective-permute-done), channel_id=1, source_target_pairs={{0,4},{1,5},{2,6},{3,7},{4,8},{5,9},{6,10},{7,11},{8,12},{9,13},{1... | collective-permute-start | bytes 221192 | tf_op jit(solution)/shard_map/ppermute | solution.py:23
  236.1 7.7 %collective-permute-start.2 = (bf16[128,288]{0,1:T(8,128)(2,1)}, bf16[128,288]{0,1:T(8,128)(2,1)S(1)}, u32[]{:S(2)}, u32[]{:S(2)}) collective-permute-start(bf16[128,288]{0,1:T(8,128)(2,1)} %collective-permute-done.1), channel_id=1, source_target_pairs={{0,4},{1,5},{2,6},{3,7},{4,8},{5,9},{6,10},{7,11},{8,12},{9,13},{1... | collective-permute-start | bytes 221192 | tf_op jit(solution)/shard_map/ppermute | solution.py:23
  243.9 10.2 %collective-permute-start.3 = (bf16[128,288]{0,1:T(8,128)(2,1)S(1)}, bf16[128,288]{0,1:T(8,128)(2,1)S(1)}, u32[]{:S(2)}, u32[]{:S(2)}) collective-permute-start(bf16[128,288]{0,1:T(8,128)(2,1)S(1)} %collective-permute-done.2), channel_id=1, source_target_pairs={{0,4},{1,5},{2,6},{3,7},{4,8},{5,9},{6,10},{7,11},{8,12},{9,13},{1... | collective-permute-start | bytes 221192 | tf_op jit(solution)/shard_map/ppermute | solution.py:23
  254.1 12.3 %collective-permute-start.4 = (bf16[128,288]{0,1:T(8,128)(2,1)S(1)}, bf16[128,288]{0,1:T(8,128)(2,1)S(1)}, u32[]{:S(2)}, u32[]{:S(2)}) collective-permute-start(bf16[128,288]{0,1:T(8,128)(2,1)S(1)} %collective-permute-done.3), channel_id=1, source_target_pairs={{0,4},{1,5},{2,6},{3,7},{4,8},{5,9},{6,10},{7,11},{8,12},{9,13},{1... | collective-permute-start | bytes 221192 | tf_op jit(solution)/shard_map/ppermute | solution.py:23
  265.3 12.3 %copy-start.7 = (bf16[2560]{0:T(1024)(128)(2,1)S(1)}, bf16[2560]{0:T(1024)(128)(2,1)}, u32[]{:S(2)}) copy-start(bf16[2560]{0:T(1024)(128)(2,1)} %param.35) | copy-start | bytes 15364
  266.3 11.3 %collective-permute-start.5 = (bf16[128,288]{0,1:T(8,128)(2,1)S(1)}, bf16[128,288]{0,1:T(8,128)(2,1)S(1)}, u32[]{:S(2)}, u32[]{:S(2)}) collective-permute-start(bf16[128,288]{0,1:T(8,128)(2,1)S(1)} %collective-permute-done.4), channel_id=1, source_target_pairs={{0,4},{1,5},{2,6},{3,7},{4,8},{5,9},{6,10},{7,11},{8,12},{9,13},{1... | collective-permute-start | bytes 221192 | tf_op jit(solution)/shard_map/ppermute | solution.py:23
  277.6 6.8 %collective-permute-start.6 = (bf16[128,288]{0,1:T(8,128)(2,1)S(1)}, bf16[128,288]{0,1:T(8,128)(2,1)S(1)}, u32[]{:S(2)}, u32[]{:S(2)}) collective-permute-start(bf16[128,288]{0,1:T(8,128)(2,1)S(1)} %collective-permute-done.5), channel_id=1, source_target_pairs={{0,4},{1,5},{2,6},{3,7},{4,8},{5,9},{6,10},{7,11},{8,12},{9,13},{1... | collective-permute-start | bytes 221192 | tf_op jit(solution)/shard_map/ppermute | solution.py:23
  323.7 4.0 copy-start.3
  336.9 4.0 copy-start.3
  434.9 50.3 %copy-start.4 = (bf16[128,2560]{1,0:T(8,128)(2,1)}, bf16[128,2560]{1,0:T(8,128)(2,1)S(1)}, u32[]{:S(2)}) copy-start(bf16[128,2560]{1,0:T(8,128)(2,1)S(1)} %fusion.59) | copy-start | bytes 1966084
  436.3 91.7 %all-gather.12.cloned.1.call-start = ((), (), s32[]{:S(2)}) async-start(), calls=%async_computation.5 | async-start | bytes 4730880 | tf_op jit(solution)/shard_map/all_gather | solution.py:193
  436.8 139.2 %all-gather.14.cloned.1.call-start = ((), (), s32[]{:S(2)}) async-start(), calls=%async_computation.6 | async-start | bytes 4730880 | tf_op jit(solution)/shard_map/all_gather | solution.py:199
  437.4 183.4 %reduce-scatter.2.cloned.1.call-start = ((), (), s32[]{:S(2)}) async-start(), calls=%async_computation.7 | async-start | bytes 3276800 | tf_op jit(solution)/shard_map/reduce_scatter | solution.py:202
  576.0 47.1 %copy-start.1 = (bf16[768,1920]{1,0:T(8,128)(2,1)S(1)}, bf16[768,1920]{1,0:T(8,128)(2,1)}, u32[]{:S(2)}) copy-start(bf16[768,1920]{1,0:T(8,128)(2,1)} %param.29) | copy-start | bytes 8847364
Sparse Core Ops, SparseCore 0:
  10.3 52.7 all-gather.5
  85.0 139.8 all-gather.9
  436.4 42.0 all-gather.7
  480.7 47.2 all-gather.11
  530.2 45.8 all-gather.13
  588.0 32.7 reduce-scatter.1
